TPU v7x, 512 devices: a whole 4x4x16 slice. The times are simulated.
512 devices in a mesh: outer: 32 (over z, x_hi), inner: 16 (over x_lo, y, core).
Axes of the slice: x: 4 (x_hi: 2, x_lo: 2; x = x_hi * 2 + x_lo), y: 4, z: 16, core: 2. Of those that a mesh axis runs over, the one named last changes fastest.
Arguments:
- queries: bfloat16 [16384, 128], P('inner'), may hold values from -150 to 150
- key_rows: bfloat16 [131072, 128], P(('outer', 'inner')), may hold values from -4.5 to 4.5
- value_rows: bfloat16 [131072, 128], P(('outer', 'inner')), may hold values from -6 to 6
Outputs:
- attended: bfloat16 [16384, 128], P('inner')
All inputs are finite; a program needn't handle non-finite values.
Results may differ from a plain program's by a relative error of at most 0.015.
Values may be sent and summed in bfloat16 or wider, within the bound.
No kernel may reach another device: no remote copies, remote signals or barrier semaphores. Data moves between devices by JAX's collectives and lax.ppermute only.
A program may use at most 64 MiB of HBM per device.

v0:
```python
import math
import jax
import jax.numpy as jnp
from jax import lax
from jax.sharding import PartitionSpec as P


def merged(part, axis, combine):
    gathered = jax.tree.map(lambda a: lax.all_gather(a, axis), part)

    def take(source):
        return jax.tree.map(lambda a: lax.dynamic_index_in_dim(a, source, 0, False), gathered)

    return lax.fori_loop(
        1, lax.axis_size(axis), lambda source, state: combine(state, take(source)), take(0)
    )


def combine_partial(left, right):
    left_sum, left_peak, left_total = left
    right_sum, right_peak, right_total = right
    joint_peak = jnp.maximum(left_peak, right_peak)
    left_factor = jnp.exp(left_peak - joint_peak)
    right_factor = jnp.exp(right_peak - joint_peak)
    joint_sum = left_sum * left_factor[:, None] + right_sum * right_factor[:, None]
    joint_total = left_total * left_factor + right_total * right_factor
    return (joint_sum, joint_peak, joint_total)


def on_device(queries, key_rows, value_rows):
    query_count, head_size = queries.shape
    score_scale = 1.0 / math.sqrt(head_size)

    def advance(running, tiles):
        weighted, row_peak, row_total = running
        key_tile, value_tile = tiles
        scores = (
            lax.dot_general(
                queries, key_tile, (((1,), (1,)), ((), ())), preferred_element_type=jnp.float32
            )
            * score_scale
        )
        new_peak = jnp.maximum(row_peak, jnp.max(scores, axis=1))
        rescale = jnp.exp(row_peak - new_peak)
        probs = jnp.exp(scores - new_peak[:, None])
        new_total = row_total * rescale + jnp.sum(probs, axis=1)
        new_weighted = weighted * rescale[:, None] + jnp.dot(
            probs.astype(jnp.bfloat16), value_tile, preferred_element_type=jnp.float32
        )
        return ((new_weighted, new_peak, new_total), None)

    start_state = (
        jnp.zeros((query_count, head_size), jnp.float32),
        jnp.full((query_count,), -1e30, jnp.float32),
        jnp.zeros((query_count,), jnp.float32),
    )
    key_part = lax.all_gather(key_rows, "inner", axis=0, tiled=True)
    value_part = lax.all_gather(value_rows, "inner", axis=0, tiled=True)
    row_count = key_part.shape[0]
    block_rows = math.gcd(row_count, 256)
    key_tiles = key_part.reshape(row_count // block_rows, block_rows, head_size)
    value_tiles = value_part.reshape(row_count // block_rows, block_rows, head_size)
    result, unused = lax.scan(advance, start_state, (key_tiles, value_tiles))
    weighted, row_peak, row_total = result
    joint_sum, joint_peak, joint_total = merged(
        (weighted, row_peak, row_total), "outer", combine_partial
    )
    attended = (joint_sum / joint_total[:, None]).astype(jnp.bfloat16)
    return attended


def solution(mesh):
    return jax.shard_map(
        on_device,
        mesh=mesh,
        in_specs=(P("inner", None), P(("outer", "inner"), None), P(("outer", "inner"), None)),
        out_specs=P("inner", None),
        check_vma=False,
    )
```

profile of v0, /device:TPU:1, one launch (start us, length us, event | category | flops | bytes accessed | tf_op | source)
XLA Modules:
  0.0 469.2 jit_solution(17336920860989906849)
XLA Ops:
  8.1 46.9 %all-gather.7.cloned.1.call-done = bf16[4096,128]{1,0:T(8,128)(2,1)} async-done(((bf16[256,128]{1,0:T(8,128)(2,1)}), bf16[4096,128]{1,0:T(8,128)(2,1)}) %all-gather.7.cloned.1.call-update) | async-done | bytes 1048592 | tf_op jit(solution)/shard_map/all_gather | solution.py:57
  55.0 42.1 %all-gather.9.cloned.1.call-done = bf16[4096,128]{1,0:T(8,128)(2,1)} async-done(((bf16[256,128]{1,0:T(8,128)(2,1)}), bf16[4096,128]{1,0:T(8,128)(2,1)}) %all-gather.9.cloned.1.call-update) | async-done | bytes 1048592 | tf_op jit(solution)/shard_map/all_gather | solution.py:58
  97.1 46.3 %while.35 = (s32[]{:T(128)}, f32[1024,128]{1,0:T(8,128)S(1)}, f32[1024]{0:T(1024)S(1)}, f32[1024]{0:T(1024)S(1)}, bf16[16,256,128]{2,1,0:T(8,128)(2,1)}, /*index...) while((s32[]{:T(128)}, f32[1024,128]{1,0:T(8,128)S(1)}, ...), condition=%wide.region_3.4_spmd.clone, body=%wide.region_0.3_spmd.clone.sunk | while | flops 136188928 | bytes 4653177 | solution.py:63
  98.6 1.4 convolution_add_fusion.2
  101.5 1.4 convolution_add_fusion.2
  104.4 1.4 convolution_add_fusion.2
  113.1 1.4 convolution_add_fusion.2
  116.0 1.4 convolution_add_fusion.2
  118.9 1.4 convolution_add_fusion.2
  121.8 1.4 convolution_add_fusion.2
  124.7 1.4 convolution_add_fusion.2
  127.6 1.4 convolution_add_fusion.2
  130.5 1.4 convolution_add_fusion.2
  144.3 63.4 %all-gather.2 = f32[32768]{0:T(1024)S(1)} all-gather(f32[1024]{0:T(1024)S(1)} %get-tuple-element.223), channel_id=4, replica_groups=mesh['outer'=32,'inner'=16] {'outer'}, dimensions={0}, use_global_device_ids=true | all-gather | bytes 135168 | tf_op jit(solution)/shard_map/all_gather | solution.py:9
  207.7 58.3 %all-gather.1 = f32[32768]{0:T(1024)S(1)} all-gather(f32[1024]{0:T(1024)S(1)} %get-tuple-element.222), channel_id=3, replica_groups=mesh['outer'=32,'inner'=16] {'outer'}, dimensions={0}, use_global_device_ids=true | all-gather | bytes 135168 | tf_op jit(solution)/shard_map/all_gather | solution.py:9
  266.1 146.1 %all-gather.11.cloned.1.call-done = f32[32768,128]{1,0:T(8,128)} async-done(((f32[1024,128]{1,0:T(8,128)}), f32[32768,128]{1,0:T(8,128)}) %all-gather.11.cloned.1.call-update) | async-done | bytes 16777232 | tf_op jit(solution)/shard_map/all_gather | solution.py:9
  413.2 48.5 %while.34 = (s32[]{:T(128)}, f32[1024,128]{1,0:T(8,128)S(1)}, f32[1024]{0:T(1024)S(1)}, f32[1024]{0:T(1024)S(1)}, f32[32,1024]{1,0:T(8,128)S(1)}, /*index=5*/f32...) while((s32[]{:T(128)}, f32[1024,128]{1,0:T(8,128)S(1)}, ...), condition=%wide.region_5.6_spmd, body=%wide.region_4.5_spmd.sunk | while | flops 399365 | bytes 1630351 | solution.py:14
  413.3 1.5 fusion.21
  414.8 1.5 fusion.21
  416.4 1.5 fusion.21
  418.0 1.5 fusion.21
  419.5 1.5 fusion.21
  421.1 1.5 fusion.21
  422.7 1.5 fusion.21
  424.2 1.5 fusion.21
  425.8 1.5 fusion.21
  427.4 1.5 fusion.21
  428.9 1.5 fusion.21
  430.5 1.5 fusion.21
  432.0 1.5 fusion.21
  433.6 1.5 fusion.21
  435.2 1.5 fusion.21
  436.7 1.5 fusion.21
  438.3 1.5 fusion.21
  439.9 1.5 fusion.21
  441.4 1.5 fusion.21
  443.0 1.5 fusion.21
  444.6 1.5 fusion.21
  446.1 1.5 fusion.21
  447.7 1.5 fusion.21
  449.3 1.5 fusion.21
  450.8 1.5 fusion.21
  452.4 1.5 fusion.21
  453.9 1.5 fusion.21
  455.5 1.5 fusion.21
  457.1 1.5 fusion.21
  458.6 1.5 fusion.21
  460.2 1.5 fusion.21
  (165 shorter events, 37.2 us)
Async XLA Ops:
  6.5 48.5 %all-gather.7.cloned.1.call-start = ((), (), s32[]{:S(2)}) async-start(), calls=%async_computation | async-start | bytes 1114112 | tf_op jit(solution)/shard_map/all_gather | solution.py:57
  7.3 89.8 %all-gather.9.cloned.1.call-start = ((), (), s32[]{:S(2)}) async-start(), calls=%async_computation.1 | async-start | bytes 1114112 | tf_op jit(solution)/shard_map/all_gather | solution.py:58
  8.0 404.1 %all-gather.11.cloned.1.call-start = ((), (), s32[]{:S(2)}) async-start(), calls=%async_computation.2 | async-start | bytes 17301504 | tf_op jit(solution)/shard_map/all_gather | solution.py:9
  143.4 0.8 copy-start
Sparse Core Ops, SparseCore 0:
  9.5 45.4 all-gather.6
  57.2 39.9 all-gather.8
  144.4 267.7 all-gather.10
where the time goes:
time: 472 us; the launch traced here: 469 us
  waiting for transfers between devices  236 us (50%)
  blocking collectives  122 us (26%)
  other arithmetic  50.8 us (11%)
  matrix products  42.5 us (9%)
  between operations  13.2 us (3%)
    all_gather x1, waiting for transfers between devices, merged(): gathered = jax.tree.map(lambda a: lax.all_gather(a, axis), part)  146 us
    all_gather x2, blocking collectives, merged(): gathered = jax.tree.map(lambda a: lax.all_gather(a, axis), part)  122 us
    all_gather x1, waiting for transfers between devices, on_device(): key_part = lax.all_gather(key_rows, 'inner', axis=0, tiled=True)  46.9 us
    add x31, other arithmetic, combine_partial(): left_sum * left_factor[:, None] + right_sum * right_factor[:, None]  46.5 us
    all_gather x1, waiting for transfers between devices, on_device(): value_part = lax.all_gather(value_rows, 'inner', axis=0, tiled=True)  42.1 us
    dot_general x16, matrix products, advance(): jnp.dot(probs.astype(jnp.bfloat16), value_tile, preferred_element_type=jn...  21.7 us
    dot_general x16, matrix products, advance(): lax.dot_general(queries, key_tile, (((1,), (1,)), ((), ())), preferred_el...  20.8 us
  transfers between devices with their start and end apart: 3, of which 3 were waited for; matrix products, arithmetic and copies ran while one was open for 0% of the time, Pallas kernels for 0%

commit v1 on v0

--- a/solution.py
+++ b/solution.py
@@ -54,7 +54,9 @@
         jnp.full((query_count,), -1e30, jnp.float32),
         jnp.zeros((query_count,), jnp.float32),
     )
-    key_part = lax.all_gather(key_rows, "inner", axis=0, tiled=True)
+    key_part = jnp.concatenate(
+        lax.all_to_all(jnp.stack([key_rows] * lax.axis_size("inner")), "inner", 0, 0), axis=0
+    )
     value_part = lax.all_gather(value_rows, "inner", axis=0, tiled=True)
     row_count = key_part.shape[0]
     block_rows = math.gcd(row_count, 256)

time: 472 us -> 430 us (0.911)
  waiting for transfers between devices: 236 us -> 180 us
  starting transfers between devices: 0.08 us -> 10.3 us
    all_gather x1 -> x0, waiting for transfers between devices: 46.9 us -> none  [on_device(): key_part = lax.all_gather(key_rows, 'inner', axis=0, tiled=True)]
    all_gather x1, waiting for transfers between devices: 42.1 us -> 19.5 us  [on_device(): value_part = lax.all_gather(value_rows, 'inner', axis=0, tiled=True)]
    all_to_all x0 -> x1, waiting for transfers between devices: none -> 15.7 us  [on_device(): lax.all_to_all(jnp.stack([key_rows] * lax.axis_size('inner')), 'inner', 0...]
    all_to_all x0 -> x1, starting transfers between devices: none -> 10.3 us  [on_device(): lax.all_to_all(jnp.stack([key_rows] * lax.axis_size('inner')), 'inner', 0...]
where the time goes in v1:
time: 430 us; the launch traced here: 427 us
  waiting for transfers between devices  180 us (42%)
  blocking collectives  123 us (29%)
  other arithmetic  50.8 us (12%)
  matrix products  41.8 us (10%)
  between operations  13.5 us (3%)
  starting transfers between devices  10.3 us (2%)
  local copies, waits for them, and re-layouts  4.5 us (1%)
    all_gather x1, waiting for transfers between devices, merged(): gathered = jax.tree.map(lambda a: lax.all_gather(a, axis), part)  145 us
    all_gather x2, blocking collectives, merged(): gathered = jax.tree.map(lambda a: lax.all_gather(a, axis), part)  123 us
    add x31, other arithmetic, combine_partial(): left_sum * left_factor[:, None] + right_sum * right_factor[:, None]  46.5 us
    dot_general x16, matrix products, advance(): jnp.dot(probs.astype(jnp.bfloat16), value_tile, preferred_element_type=jn...  21.7 us
    dot_general x16, matrix products, advance(): lax.dot_general(queries, key_tile, (((1,), (1,)), ((), ())), preferred_el...  20.1 us
    all_gather x1, waiting for transfers between devices, on_device(): value_part = lax.all_gather(value_rows, 'inner', axis=0, tiled=True)  19.5 us
    all_to_all x1, waiting for transfers between devices, on_device(): lax.all_to_all(jnp.stack([key_rows] * lax.axis_size('inner')), 'inner', 0...  15.7 us
    all_to_all x1, starting transfers between devices, on_device(): lax.all_to_all(jnp.stack([key_rows] * lax.axis_size('inner')), 'inner', 0...  10.3 us
  transfers between devices with their start and end apart: 3, of which 3 were waited for; matrix products, arithmetic and copies ran while one was open for 0% of the time, Pallas kernels for 0%

profile of v1, /device:TPU:1, one launch (start us, length us, event | category | flops | bytes accessed | tf_op | source)
XLA Modules:
  0.0 426.6 jit_solution(2505914010441884048)
XLA Ops:
  7.3 2.1 stack.2
  9.3 10.3 %all-to-all-start = ((bf16[16,256,128]{2,1,0:T(8,128)(2,1)}), bf16[16,256,128]{2,1,0:T(8,128)(2,1)S(1)}, u32[]{:S(2)}, u32[]{:S(2)}) async-start(bf16[16,256,128]{2,1,0:T(8,128)(2,1)} %stack.2), calls=%async_computation | async-start | bytes 2097152 | tf_op jit(solution)/shard_map/all_to_all | solution.py:58
  19.7 15.7 %all-to-all-done = bf16[16,256,128]{2,1,0:T(8,128)(2,1)S(1)} async-done(((bf16[16,256,128]{2,1,0:T(8,128)(2,1)}), bf16[16,256,128]{2,1,0:T(8,128)(2,1)S(1)}, u32[]{:S(2)}, u32[]{:S(2)}) %all-to-all-start) | async-done | bytes 1048608 | tf_op jit(solution)/shard_map/all_to_all | solution.py:58
  35.4 19.5 %all-gather.6.cloned.1.call-done = bf16[4096,128]{1,0:T(8,128)(2,1)} async-done(((bf16[256,128]{1,0:T(8,128)(2,1)}), bf16[4096,128]{1,0:T(8,128)(2,1)}) %all-gather.6.cloned.1.call-update) | async-done | bytes 1048592 | tf_op jit(solution)/shard_map/all_gather | solution.py:60
  54.9 45.7 %while.35 = (s32[]{:T(128)}, f32[1024,128]{1,0:T(8,128)S(1)}, f32[1024]{0:T(1024)S(1)}, f32[1024]{0:T(1024)S(1)}, bf16[16,256,128]{2,1,0:T(8,128)(2,1)S(1)}, /*i...) while((s32[]{:T(128)}, f32[1024,128]{1,0:T(8,128)S(1)}, ...), condition=%wide.region_3.4_spmd.clone, body=%wide.region_0.3_spmd.clone.sunk | while | flops 136188928 | bytes 4653177 | solution.py:65
  56.4 1.4 convolution_add_fusion.2
  59.2 1.4 convolution_add_fusion.2
  62.1 1.4 convolution_add_fusion.2
  64.9 1.4 convolution_add_fusion.2
  67.8 1.4 convolution_add_fusion.2
  70.6 1.4 convolution_add_fusion.2
  84.9 1.4 convolution_add_fusion.2
  87.8 1.4 convolution_add_fusion.2
  101.4 65.3 %all-gather.2 = f32[32768]{0:T(1024)S(1)} all-gather(f32[1024]{0:T(1024)S(1)} %get-tuple-element.223), channel_id=4, replica_groups=mesh['outer'=32,'inner'=16] {'outer'}, dimensions={0}, use_global_device_ids=true | all-gather | bytes 135168 | tf_op jit(solution)/shard_map/all_gather | solution.py:9
  166.8 58.0 %all-gather.1 = f32[32768]{0:T(1024)S(1)} all-gather(f32[1024]{0:T(1024)S(1)} %get-tuple-element.222), channel_id=3, replica_groups=mesh['outer'=32,'inner'=16] {'outer'}, dimensions={0}, use_global_device_ids=true | all-gather | bytes 135168 | tf_op jit(solution)/shard_map/all_gather | solution.py:9
  224.8 144.5 %all-gather.8.cloned.1.call-done = f32[32768,128]{1,0:T(8,128)} async-done(((f32[1024,128]{1,0:T(8,128)}), f32[32768,128]{1,0:T(8,128)}) %all-gather.8.cloned.1.call-update) | async-done | bytes 16777232 | tf_op jit(solution)/shard_map/all_gather | solution.py:9
  370.4 48.5 %while.34 = (s32[]{:T(128)}, f32[1024,128]{1,0:T(8,128)S(1)}, f32[1024]{0:T(1024)S(1)}, f32[1024]{0:T(1024)S(1)}, f32[32,1024]{1,0:T(8,128)S(1)}, /*index=5*/f32...) while((s32[]{:T(128)}, f32[1024,128]{1,0:T(8,128)S(1)}, ...), condition=%wide.region_5.6_spmd, body=%wide.region_4.5_spmd.sunk | while | flops 399365 | bytes 1630351 | solution.py:14
  370.4 1.5 fusion.21
  372.0 1.5 fusion.21
  373.6 1.5 fusion.21
  375.1 1.5 fusion.21
  376.7 1.5 fusion.21
  378.2 1.5 fusion.21
  379.8 1.5 fusion.21
  381.4 1.5 fusion.21
  382.9 1.5 fusion.21
  384.5 1.5 fusion.21
  386.1 1.5 fusion.21
  387.6 1.5 fusion.21
  389.2 1.5 fusion.21
  390.8 1.5 fusion.21
  392.3 1.5 fusion.21
  393.9 1.5 fusion.21
  395.5 1.5 fusion.21
  397.0 1.5 fusion.21
  398.6 1.5 fusion.21
  400.1 1.5 fusion.21
  401.7 1.5 fusion.21
  403.3 1.5 fusion.21
  404.8 1.5 fusion.21
  406.4 1.5 fusion.21
  408.0 1.5 fusion.21
  409.5 1.5 fusion.21
  411.1 1.5 fusion.21
  412.7 1.5 fusion.21
  414.2 1.5 fusion.21
  415.8 1.5 fusion.21
  417.4 1.5 fusion.21
  (165 shorter events, 38.5 us)
Async XLA Ops:
  6.5 48.4 %all-gather.6.cloned.1.call-start = ((), (), s32[]{:S(2)}) async-start(), calls=%async_computation.1 | async-start | bytes 1114112 | tf_op jit(solution)/shard_map/all_gather | solution.py:60
  9.3 26.0 %all-to-all-start = ((bf16[16,256,128]{2,1,0:T(8,128)(2,1)}), bf16[16,256,128]{2,1,0:T(8,128)(2,1)S(1)}, u32[]{:S(2)}, u32[]{:S(2)}) async-start(bf16[16,256,128]{2,1,0:T(8,128)(2,1)} %stack.2), calls=%async_computation | async-start | bytes 2097152 | tf_op jit(solution)/shard_map/all_to_all | solution.py:58
  19.6 349.7 %all-gather.8.cloned.1.call-start = ((), (), s32[]{:S(2)}) async-start(), calls=%async_computation.2 | async-start | bytes 17301504 | tf_op jit(solution)/shard_map/all_gather | solution.py:9
  100.6 0.8 copy-start
Sparse Core Ops, SparseCore 0:
  9.5 45.3 all-gather.5
  101.5 267.7 all-gather.7
